TPU v7x, 256 devices: a whole 4x4x8 slice. The times are simulated.
256 devices in a mesh: grp: 8 (over y_hi, x), dom: 32 (over y_lo, z, core).
Axes of the slice: x: 4, y: 4 (y_hi: 2, y_lo: 2; y = y_hi * 2 + y_lo), z: 8, core: 2. Of those that a mesh axis runs over, the one named last changes fastest.
Arguments:
- fine_matrix_blocks: bfloat16 [16384, 64, 768], P(('grp', 'dom')), may hold values from -0.21875 to 0.21875
- prolongator: bfloat16 [16384, 64, 64], P(('grp', 'dom')), may hold values from -1.5 to 1.5
- block_columns: int32 [16384, 12], P(('grp', 'dom')), may hold values from 0 to 16383, as said below
- block_aggregates: int32 [16384, 12], P(('grp', 'dom')), may hold values from 0 to 1023, as said below
- live_counts: int32 [256], P(('grp', 'dom')), may hold values from 16 to 64, as said below
Outputs:
- coarse_operator: float32 [1024, 64, 768], P('dom')
Inputs may be any that keep to these rules, and one draw needn't show every extreme that they name: live_counts[p] counts the first slots of partition p that hold block rows; some partition has 64 and some has 16. `block_columns`: entry 0 of row i is i itself. For a live row of partition p, every entry is a live row of partition p - 1, p or p + 1 (only partitions that exist); entries may repeat, and repeated blocks add. block_aggregates[i, k] is the aggregate of row block_columns[i, k]. Every row of partition p, with g = p // 32 and q = p % 32, has an aggregate from (((q + 4 * g) % 32) * 8 + g) * 4 to that number plus 4 - 1.
All inputs are finite; a program needn't handle non-finite values.
Results may differ from a plain program's by a relative error of at most 0.0029.
Values may be sent and summed in bfloat16 or wider, within the bound.
No kernel may reach another device: no remote copies, remote signals or barrier semaphores. Data moves between devices by JAX's collectives and lax.ppermute only.
A program may use at most 192 MiB of HBM per device.

v0:
```python
import jax
import jax.numpy as jnp
from jax import lax
from jax.sharding import PartitionSpec as P

AGG_DEV = 4


def extended(block, sides, width):
    for axis, dim in sides:
        count = lax.axis_size(axis)
        forward = [(i, i + 1) for i in range(count - 1)]
        backward = [(target, source) for source, target in forward]
        low = lax.ppermute(
            lax.slice_in_dim(block, block.shape[dim] - width, None, axis=dim), axis, forward
        )
        high = lax.ppermute(lax.slice_in_dim(block, 0, width, axis=dim), axis, backward)
        block = jnp.concatenate([low, block, high], axis=dim)
    return block


def passed_along(value, axis, by):
    peers = lax.axis_size(axis)
    return lax.ppermute(value, axis, [(i, (i + by) % peers) for i in range(peers)])


def local(fine_matrix_blocks, prolongator, block_columns, block_aggregates, live_counts):
    capacity = fine_matrix_blocks.shape[0]
    block_width = prolongator.shape[1]
    row_blocks = block_columns.shape[1]
    slot_width = 3 * AGG_DEV
    position = lax.axis_index(("grp", "dom"))
    ghosts = extended(prolongator, ((("grp", "dom"), 0),), capacity)
    local_rows = block_columns - (position - 1) * capacity
    gathered = jnp.take(ghosts, local_rows, axis=0)
    matrix_view = fine_matrix_blocks.reshape(capacity, block_width, row_blocks, block_width)
    products = jnp.einsum(
        "ixky,ikyz->ixkz", matrix_view, gathered, preferred_element_type=jnp.float32
    )
    coarse_slot = AGG_DEV * (local_rows // capacity) + block_aggregates % AGG_DEV
    live_rows = jnp.arange(capacity) < live_counts[0]
    slot_select = (coarse_slot[:, :, None] == jnp.arange(slot_width)[None, None, :]) & live_rows[
        :, None, None
    ]
    row_sums = jnp.einsum(
        "ikt,ixkz->ixtz", slot_select.astype(jnp.float32), products, precision=lax.Precision.HIGHEST
    )
    row_sums = row_sums.astype(jnp.bfloat16).reshape(
        capacity * block_width, slot_width * block_width
    )
    row_select = (block_aggregates[:, 0:1] % AGG_DEV == jnp.arange(AGG_DEV)[None, :]) & live_rows[
        :, None
    ]
    spread = row_select.astype(jnp.bfloat16)[:, None, :, None] * prolongator[:, :, None, :]
    spread = spread.reshape(capacity * block_width, AGG_DEV * block_width)
    coarse = lax.dot_general(
        spread, row_sums, (((0,), (0,)), ((), ())), preferred_element_type=jnp.float32
    )
    groups_count = lax.axis_size("grp")
    step_stride = lax.axis_size("dom") // groups_count
    group_index = lax.axis_index("grp")
    rotated = coarse
    for bit_number in range(groups_count.bit_length() - 1):
        arrived = passed_along(rotated, "dom", step_stride << bit_number)
        rotated = jnp.where((group_index >> bit_number) % 2 == 1, arrived, rotated)
    result = lax.all_gather(rotated[None], "grp", axis=0, tiled=True)
    return result.reshape(groups_count * AGG_DEV, block_width, slot_width * block_width)


def solution(mesh):
    return jax.shard_map(
        local,
        mesh=mesh,
        in_specs=(
            P(("grp", "dom"), None, None),
            P(("grp", "dom"), None, None),
            P(("grp", "dom"), None),
            P(("grp", "dom"), None),
            P(("grp", "dom")),
        ),
        out_specs=P("dom", None, None),
        check_vma=False,
    )
```

profile of v0, /device:TPU:1, one launch (start us, length us, event | category | flops | bytes accessed | tf_op | source)
XLA Modules:
  0.0 395.2 jit_solution(863986176305773852)
XLA Ops:
  6.5 0.0 copy-start.1
  6.5 0.0 all-gather.3.cloned.1.call-start
  6.5 5.0 %collective-permute-start = (bf16[64,64,64]{2,1,0:T(8,128)(2,1)}, bf16[64,64,64]{2,1,0:T(8,128)(2,1)S(1)}, u32[]{:S(2)}, u32[]{:S(2)}) collective-permute-start(bf16[64,64,64]{2,1,0:T(8,128)(2,1)} %param.6), channel_id=1, source_target_pairs={{0,1},{1,2},{2,3},{3,4},{4,5},{5,6},{6,7},{7,8},{8,9},{9,10},{10,1... | collective-permute-start | bytes 1572872 | tf_op jit(solution)/shard_map/ppermute | solution.py:14
  11.6 1.9 collective-permute-start.1
  13.5 0.7 compare_and_fusion
  14.2 0.7 fusion.17
  15.0 0.7 fusion.22
  15.7 0.1 copy.14
  15.8 0.1 reshape.79
  15.9 0.1 copy.13
  16.0 19.7 %reshape.74 = bf16[64,64,12,64]{3,2,1,0:T(8,128)(2,1)} reshape(bf16[64,64,768]{2,1,0:T(8,128)(2,1)} %param.5) | data formatting | bytes 12582912 | tf_op jit(solution)/shard_map/reshape | solution.py:36
  35.7 0.1 copy.17
  36.4 0.1 copy.12
  36.5 0.0 copy-done.1
  36.6 4.2 %broadcast_multiply_fusion = bf16[64,64,4,64]{3,2,1,0:T(4,128)(2,1)} fusion(bf16[64,64,64]{2,1,0:T(8,128)(2,1)S(1)} %copy-done.1, bf16[64,4]{1,0:T(8,128)(2,1)S(1)} %copy.12), kind=kLoop, calls=%fused_computation.9 | loop fusion | flops 1048576 | bytes 2621952 | tf_op jit(solution)/shard_map/mul | solution.py:54
  40.8 7.0 %mul.38 = bf16[4096,256]{1,0:T(8,128)(2,1)} reshape(bf16[64,64,4,64]{3,2,1,0:T(4,128)(2,1)} %broadcast_multiply_fusion) | data formatting | bytes 4194304 | tf_op jit(solution)/shard_map/mul | solution.py:54
  47.7 0.0 collective-permute-done
  47.8 0.0 copy-start.2
  47.8 1.0 copy-done.2
  48.7 0.0 collective-permute-done.1
  48.7 2.2 pad_maximum_fusion
  51.0 18.2 %gather_fusion = bf16[768,64,64]{2,1,0:T(8,128)(2,1)} fusion(bf16[192,64,64]{2,1,0:T(8,128)(2,1)S(1)} %pad_maximum_fusion, s32[1024]{0:T(1024)S(1)} %pad_clamp_fusion), kind=kCustom, calls=%fused_computation | custom fusion | bytes 12585984 | tf_op jit(solution)/shard_map/jit(_take)/gather | solution.py:35
  69.1 16.6 %copy.15 = bf16[64,12,64,64]{2,3,1,0:T(8,128)(2,1)} copy(bf16[64,12,64,64]{3,2,1,0:T(8,128)(2,1)} %bitcast.18) | data formatting | bytes 12582912 | tf_op jit(solution)/shard_map/jit(_take)/gather | solution.py:35
  85.8 21.7 %fusion.4 = f32[64,64,12,64]{1,3,2,0:T(8,128)} fusion(bf16[64,64,12,64]{3,2,1,0:T(8,128)(2,1)} %reshape.74, bf16[64,12,64,64]{2,3,1,0:T(8,128)(2,1)} %copy.15, pred[64,12]{1,0:T(8,128)(4,1)S(1)} %copy.13), kind=kOutput, calls=%fused_computation.6 | convolution fusion | flops 405798912 | bytes 25166592 | tf_op jit(solution)/shard_map/ixky,ikyz->ixkz/dot_general | solution.py:37
  107.5 31.1 %copy.18 = f32[64,64,12,64]{3,2,1,0:T(8,128)} copy(f32[64,64,12,64]{1,3,2,0:T(8,128)} %fusion.4) | data formatting | bytes 25165824 | tf_op jit(solution)/shard_map/ixky,ikyz->ixkz/transpose | solution.py:37
  138.6 25.0 %convert_bitcast_fusion = bf16[64,64,12,64]{3,2,1,0:T(8,128)(2,1)} fusion(f32[64,64,12,64]{3,2,1,0:T(8,128)} %copy.18, s32[64,12]{1,0:T(8,128)S(1)} %copy.17, pred[64]{0:T(512)(128)(4,1)S(1)} %iota_compare_fusion.2), kind=kOutput, calls=%fused_computation.1 | convolution fusion | flops 456148992 | bytes 18877504 | tf_op jit(solution)/shard_map/ikt,ixkz->ixtz/dot_general | solution.py:45
  163.5 0.0 copy-start
  163.5 20.9 %reshape.90 = bf16[4096,768]{1,0:T(8,128)(2,1)} reshape(bf16[64,64,12,64]{3,2,1,0:T(8,128)(2,1)} %convert_bitcast_fusion) | data formatting | bytes 12582912 | tf_op jit(solution)/shard_map/reshape | solution.py:48
  184.4 0.0 copy-done
  184.4 4.6 %fusion.25 = f32[256,768]{1,0:T(8,128)S(1)} fusion(bf16[4096,256]{1,0:T(8,128)(2,1)S(1)} %copy-done, bf16[4096,768]{1,0:T(8,128)(2,1)} %reshape.90), kind=kOutput, calls=%fused_computation.44 | convolution fusion | flops 1610612736 | bytes 9175040 | tf_op jit(solution)/shard_map/dot_general | solution.py:56
  189.0 3.3 collective-permute-start.2
  192.3 36.2 %collective-permute-done.2 = f32[256,768]{1,0:T(8,128)S(1)} collective-permute-done((f32[256,768]{1,0:T(8,128)S(1)}, f32[256,768]{1,0:T(8,128)S(1)}, u32[]{:S(2)}, u32[]{:S(2)}) %collective-permute-start.2) | collective-permute-done | bytes 786464 | tf_op jit(solution)/shard_map/ppermute | solution.py:24
  228.5 0.1 broadcast_select_fusion
  228.6 0.1 collective-permute-start.3
  228.7 39.8 %collective-permute-done.3 = f32[256,768]{1,0:T(8,128)S(1)} collective-permute-done((f32[256,768]{1,0:T(8,128)S(1)}, f32[256,768]{1,0:T(8,128)S(1)}, u32[]{:S(2)}, u32[]{:S(2)}) %collective-permute-start.3) | collective-permute-done | bytes 786464 | tf_op jit(solution)/shard_map/ppermute | solution.py:24
  268.6 0.1 broadcast_select_fusion.1
  268.7 0.1 collective-permute-start.4
  268.8 17.5 %collective-permute-done.4 = f32[256,768]{1,0:T(8,128)S(1)} collective-permute-done((f32[256,768]{1,0:T(8,128)S(1)}, f32[256,768]{1,0:T(8,128)S(1)}, u32[]{:S(2)}, u32[]{:S(2)}) %collective-permute-start.4) | collective-permute-done | bytes 786464 | tf_op jit(solution)/shard_map/ppermute | solution.py:24
  286.3 1.0 broadcast_select_fusion.2
  287.3 0.0 all-gather.3.cloned.1.call-update
  287.3 94.9 %all-gather.3.cloned.1.call-done = f32[2048,768]{1,0:T(8,128)} async-done(((f32[256,768]{1,0:T(8,128)}), f32[2048,768]{1,0:T(8,128)}) %all-gather.3.cloned.1.call-update) | async-done | bytes 6291472 | tf_op jit(solution)/shard_map/all_gather | solution.py:66
  382.2 6.2 %copy.28 = f32[32,64,768]{2,1,0:T(8,128)} copy(f32[32,64,768]{2,1,0:T(8,128)} %bitcast.19) | data formatting | bytes 12582912
  (3 shorter events, 0.0 us)
Async XLA Ops:
  6.5 30.0 %copy-start.1 = (bf16[64,64,64]{2,1,0:T(8,128)(2,1)S(1)}, bf16[64,64,64]{2,1,0:T(8,128)(2,1)}, u32[]{:S(2)}) copy-start(bf16[64,64,64]{2,1,0:T(8,128)(2,1)} %param.6) | copy-start | bytes 1572868
  6.5 375.7 %all-gather.3.cloned.1.call-start = ((), (), s32[]{:S(2)}) async-start(), calls=%async_computation | async-start | bytes 7077888 | tf_op jit(solution)/shard_map/all_gather | solution.py:66
  6.5 41.2 %collective-permute-start = (bf16[64,64,64]{2,1,0:T(8,128)(2,1)}, bf16[64,64,64]{2,1,0:T(8,128)(2,1)S(1)}, u32[]{:S(2)}, u32[]{:S(2)}) collective-permute-start(bf16[64,64,64]{2,1,0:T(8,128)(2,1)} %param.6), channel_id=1, source_target_pairs={{0,1},{1,2},{2,3},{3,4},{4,5},{5,6},{6,7},{7,8},{8,9},{9,10},{10,1... | collective-permute-start | bytes 1572872 | tf_op jit(solution)/shard_map/ppermute | solution.py:14
  11.6 37.1 %collective-permute-start.1 = (bf16[64,64,64]{2,1,0:T(8,128)(2,1)}, bf16[64,64,64]{2,1,0:T(8,128)(2,1)}, u32[]{:S(2)}, u32[]{:S(2)}) collective-permute-start(bf16[64,64,64]{2,1,0:T(8,128)(2,1)} %param.6), channel_id=1, source_target_pairs={{1,0},{2,1},{3,2},{4,3},{5,4},{6,5},{7,6},{8,7},{9,8},{10,9},{11,1... | collective-permute-start | bytes 1572872 | tf_op jit(solution)/shard_map/ppermute | solution.py:17
  47.8 1.0 copy-start.2
  163.5 20.9 %copy-start = (bf16[4096,256]{1,0:T(8,128)(2,1)S(1)}, bf16[4096,256]{1,0:T(8,128)(2,1)}, u32[]{:S(2)}) copy-start(bf16[4096,256]{1,0:T(8,128)(2,1)} %mul.38) | copy-start | bytes 6291460
  189.0 39.5 %collective-permute-start.2 = (f32[256,768]{1,0:T(8,128)S(1)}, f32[256,768]{1,0:T(8,128)S(1)}, u32[]{:S(2)}, u32[]{:S(2)}) collective-permute-start(f32[256,768]{1,0:T(8,128)S(1)} %fusion.25), channel_id=1, source_target_pairs={{0,4},{1,5},{2,6},{3,7},{4,8},{5,9},{6,10},{7,11},{8,12},{9,13},{1... | collective-permute-start | bytes 2359304 | tf_op jit(solution)/shard_map/ppermute | solution.py:24
  228.6 39.9 %collective-permute-start.3 = (f32[256,768]{1,0:T(8,128)S(1)}, f32[256,768]{1,0:T(8,128)S(1)}, u32[]{:S(2)}, u32[]{:S(2)}) collective-permute-start(f32[256,768]{1,0:T(8,128)S(1)} %broadcast_select_fusion), channel_id=1, source_target_pairs={{0,8},{1,9},{2,10},{3,11},{4,12},{5,13},{6,14},{7,15},{8,16},{9,17... | collective-permute-start | bytes 2359304 | tf_op jit(solution)/shard_map/ppermute | solution.py:24
  268.7 17.6 %collective-permute-start.4 = (f32[256,768]{1,0:T(8,128)S(1)}, f32[256,768]{1,0:T(8,128)S(1)}, u32[]{:S(2)}, u32[]{:S(2)}) collective-permute-start(f32[256,768]{1,0:T(8,128)S(1)} %broadcast_select_fusion.1), channel_id=1, source_target_pairs={{0,16},{1,17},{2,18},{3,19},{4,20},{5,21},{6,22},{7,23},{8,24},{9,... | collective-permute-start | bytes 2359304 | tf_op jit(solution)/shard_map/ppermute | solution.py:24
Sparse Core Ops, SparseCore 0:
  287.4 94.7 all-gather.2
where the time goes:
time: 398 us; the launch traced here: 395 us
  waiting for transfers between devices  188 us (47%)
  local copies, waits for them, and re-layouts  121 us (30%)
  matrix products  51.3 us (13%)
  between operations  14.2 us (4%)
  starting transfers between devices  10.4 us (3%)
  other arithmetic  9.74 us (2%)
    all_gather x1, waiting for transfers between devices, local(): result = lax.all_gather(rotated[None], 'grp', axis=0, tiled=True)  94.9 us
    ppermute x3, waiting for transfers between devices, passed_along(): lax.ppermute(value, axis, [(i, (i + by) % peers) for i in range(peers)])  93.6 us
    gather x2, local copies, waits for them, and re-layouts, local(): gathered = jnp.take(ghosts, local_rows, axis=0)  34.8 us
    transpose x1, local copies, waits for them, and re-layouts, local(): jnp.einsum('ixky,ikyz->ixkz', matrix_view, gathered, preferred_element_ty...  31.1 us
    dot_general x1, matrix products, local(): jnp.einsum('ikt,ixkz->ixtz', slot_select.astype(jnp.float32), products, p...  25 us
    dot_general x1, matrix products, local(): jnp.einsum('ixky,ikyz->ixkz', matrix_view, gathered, preferred_element_ty...  21.7 us
    reshape x1, local copies, waits for them, and re-layouts, local(): row_sums.astype(jnp.bfloat16)  20.9 us
    reshape x1, local copies, waits for them, and re-layouts, local(): fine_matrix_blocks.reshape(capacity, block_width, row_blocks, block_width)  19.7 us
  transfers between devices with their start and end apart: 6, of which 4 were waited for; matrix products, arithmetic and copies ran while one was open for 8% of the time, Pallas kernels for 0%

commit v1 on v0

--- a/solution.py
+++ b/solution.py
@@ -63,7 +63,9 @@
     for bit_number in range(groups_count.bit_length() - 1):
         arrived = passed_along(rotated, "dom", step_stride << bit_number)
         rotated = jnp.where((group_index >> bit_number) % 2 == 1, arrived, rotated)
-    result = lax.all_gather(rotated[None], "grp", axis=0, tiled=True)
+    result = jnp.concatenate(
+        lax.all_to_all(jnp.stack([rotated[None]] * lax.axis_size("grp")), "grp", 0, 0), axis=0
+    )
     return result.reshape(groups_count * AGG_DEV, block_width, slot_width * block_width)
 
 

time: 398 us -> 368 us (0.925)
  the two profiles are of different devices: /device:TPU:1 before, /device:TPU:32 now
where the time goes in v1:
time: 368 us; the launch traced here: 365 us
  local copies, waits for them, and re-layouts  118 us (32%)
  waiting for transfers between devices  85.7 us (23%)
  blocking collectives  80 us (22%)
  matrix products  51.3 us (14%)
  starting transfers between devices  20.3 us (6%)
  other arithmetic  8.86 us (2%)
    ppermute x3, waiting for transfers between devices, passed_along(): lax.ppermute(value, axis, [(i, (i + by) % peers) for i in range(peers)])  85.7 us
    all_to_all x1, blocking collectives, local(): lax.all_to_all(jnp.stack([rotated[None]] * lax.axis_size('grp')), 'grp',...  80 us
    gather x2, local copies, waits for them, and re-layouts, local(): gathered = jnp.take(ghosts, local_rows, axis=0)  34.8 us
    transpose x1, local copies, waits for them, and re-layouts, local(): jnp.einsum('ixky,ikyz->ixkz', matrix_view, gathered, preferred_element_ty...  31.1 us
    dot_general x1, matrix products, local(): jnp.einsum('ikt,ixkz->ixtz', slot_select.astype(jnp.float32), products, p...  25 us
    dot_general x1, matrix products, local(): jnp.einsum('ixky,ikyz->ixkz', matrix_view, gathered, preferred_element_ty...  21.7 us
    reshape x1, local copies, waits for them, and re-layouts, local(): row_sums.astype(jnp.bfloat16)  20.9 us
    reshape x1, local copies, waits for them, and re-layouts, local(): fine_matrix_blocks.reshape(capacity, block_width, row_blocks, block_width)  19.7 us
  transfers between devices with their start and end apart: 5, of which 3 were waited for; matrix products, arithmetic and copies ran while one was open for 9% of the time, Pallas kernels for 0%

profile of v1, /device:TPU:32, one launch (start us, length us, event | category | flops | bytes accessed | tf_op | source)
XLA Modules:
  0.0 365.0 jit_solution(12219956924152378064)
XLA Ops:
  0.0 0.0 copy-start.1
  0.0 2.0 collective-permute-start
  2.1 3.6 collective-permute-start.1
  5.7 0.7 compare_and_fusion
  6.4 0.7 fusion.17
  7.2 0.7 fusion.22
  7.8 0.1 copy.21
  7.9 0.1 reshape.77
  8.0 0.1 copy.20
  8.2 19.7 %reshape.73 = bf16[64,64,12,64]{3,2,1,0:T(8,128)(2,1)} reshape(bf16[64,64,768]{2,1,0:T(8,128)(2,1)} %param.5) | data formatting | bytes 12582912 | tf_op jit(solution)/shard_map/reshape | solution.py:36
  27.9 0.1 copy.24
  28.6 0.1 copy.19
  28.8 0.0 copy-done.1
  28.8 4.2 %broadcast_multiply_fusion = bf16[64,64,4,64]{3,2,1,0:T(4,128)(2,1)} fusion(bf16[64,64,64]{2,1,0:T(8,128)(2,1)S(1)} %copy-done.1, bf16[64,4]{1,0:T(8,128)(2,1)S(1)} %copy.19), kind=kLoop, calls=%fused_computation.9 | loop fusion | flops 1048576 | bytes 2621952 | tf_op jit(solution)/shard_map/mul | solution.py:54
  33.0 7.0 %mul.38 = bf16[4096,256]{1,0:T(8,128)(2,1)} reshape(bf16[64,64,4,64]{3,2,1,0:T(4,128)(2,1)} %broadcast_multiply_fusion) | data formatting | bytes 4194304 | tf_op jit(solution)/shard_map/mul | solution.py:54
  40.0 0.0 collective-permute-done
  40.0 0.0 copy-start.2
  40.0 1.0 copy-done.2
  40.9 0.0 collective-permute-done.1
  40.9 2.2 pad_maximum_fusion
  43.2 18.2 %gather_fusion = bf16[768,64,64]{2,1,0:T(8,128)(2,1)} fusion(bf16[192,64,64]{2,1,0:T(8,128)(2,1)S(1)} %pad_maximum_fusion, s32[1024]{0:T(1024)S(1)} %pad_clamp_fusion), kind=kCustom, calls=%fused_computation | custom fusion | bytes 12585984 | tf_op jit(solution)/shard_map/jit(_take)/gather | solution.py:35
  61.3 16.6 %copy.22 = bf16[64,12,64,64]{2,3,1,0:T(8,128)(2,1)} copy(bf16[64,12,64,64]{3,2,1,0:T(8,128)(2,1)} %bitcast.18) | data formatting | bytes 12582912 | tf_op jit(solution)/shard_map/jit(_take)/gather | solution.py:35
  78.0 21.7 %fusion.4 = f32[64,64,12,64]{1,3,2,0:T(8,128)} fusion(bf16[64,64,12,64]{3,2,1,0:T(8,128)(2,1)} %reshape.73, bf16[64,12,64,64]{2,3,1,0:T(8,128)(2,1)} %copy.22, pred[64,12]{1,0:T(8,128)(4,1)S(1)} %copy.20), kind=kOutput, calls=%fused_computation.6 | convolution fusion | flops 405798912 | bytes 25166592 | tf_op jit(solution)/shard_map/ixky,ikyz->ixkz/dot_general | solution.py:37
  99.7 31.1 %copy.25 = f32[64,64,12,64]{3,2,1,0:T(8,128)} copy(f32[64,64,12,64]{1,3,2,0:T(8,128)} %fusion.4) | data formatting | bytes 25165824 | tf_op jit(solution)/shard_map/ixky,ikyz->ixkz/transpose | solution.py:37
  130.8 25.0 %convert_bitcast_fusion = bf16[64,64,12,64]{3,2,1,0:T(8,128)(2,1)} fusion(f32[64,64,12,64]{3,2,1,0:T(8,128)} %copy.25, s32[64,12]{1,0:T(8,128)S(1)} %copy.24, pred[64]{0:T(512)(128)(4,1)S(1)} %iota_compare_fusion.2), kind=kOutput, calls=%fused_computation.1 | convolution fusion | flops 456148992 | bytes 18877504 | tf_op jit(solution)/shard_map/ikt,ixkz->ixtz/dot_general | solution.py:45
  155.8 0.0 copy-start
  155.8 20.9 %reshape.86 = bf16[4096,768]{1,0:T(8,128)(2,1)} reshape(bf16[64,64,12,64]{3,2,1,0:T(8,128)(2,1)} %convert_bitcast_fusion) | data formatting | bytes 12582912 | tf_op jit(solution)/shard_map/reshape | solution.py:48
  176.7 0.0 copy-done
  176.7 4.6 %fusion.25 = f32[256,768]{1,0:T(8,128)S(1)} fusion(bf16[4096,256]{1,0:T(8,128)(2,1)S(1)} %copy-done, bf16[4096,768]{1,0:T(8,128)(2,1)} %reshape.86), kind=kOutput, calls=%fused_computation.44 | convolution fusion | flops 1610612736 | bytes 9175040 | tf_op jit(solution)/shard_map/dot_general | solution.py:56
  181.3 3.6 collective-permute-start.2
  184.8 34.8 %collective-permute-done.2 = f32[256,768]{1,0:T(8,128)S(1)} collective-permute-done((f32[256,768]{1,0:T(8,128)S(1)}, f32[256,768]{1,0:T(8,128)S(1)}, u32[]{:S(2)}, u32[]{:S(2)}) %collective-permute-start.2) | collective-permute-done | bytes 786464 | tf_op jit(solution)/shard_map/ppermute | solution.py:24
  219.7 0.1 broadcast_select_fusion
  219.7 5.0 %collective-permute-start.3 = (f32[256,768]{1,0:T(8,128)S(1)}, f32[256,768]{1,0:T(8,128)S(1)}, u32[]{:S(2)}, u32[]{:S(2)}) collective-permute-start(f32[256,768]{1,0:T(8,128)S(1)} %broadcast_select_fusion), channel_id=1, source_target_pairs={{0,8},{1,9},{2,10},{3,11},{4,12},{5,13},{6,14},{7,15},{8,16},{9,17... | collective-permute-start | bytes 2359304 | tf_op jit(solution)/shard_map/ppermute | solution.py:24
  224.7 33.2 %collective-permute-done.3 = f32[256,768]{1,0:T(8,128)S(1)} collective-permute-done((f32[256,768]{1,0:T(8,128)S(1)}, f32[256,768]{1,0:T(8,128)S(1)}, u32[]{:S(2)}, u32[]{:S(2)}) %collective-permute-start.3) | collective-permute-done | bytes 786464 | tf_op jit(solution)/shard_map/ppermute | solution.py:24
  258.0 0.1 broadcast_select_fusion.1
  258.1 6.1 %collective-permute-start.4 = (f32[256,768]{1,0:T(8,128)S(1)}, f32[256,768]{1,0:T(8,128)S(1)}, u32[]{:S(2)}, u32[]{:S(2)}) collective-permute-start(f32[256,768]{1,0:T(8,128)S(1)} %broadcast_select_fusion.1), channel_id=1, source_target_pairs={{0,16},{1,17},{2,18},{3,19},{4,20},{5,21},{6,22},{7,23},{8,24},{9,... | collective-permute-start | bytes 2359304 | tf_op jit(solution)/shard_map/ppermute | solution.py:24
  264.1 17.6 %collective-permute-done.4 = f32[256,768]{1,0:T(8,128)S(1)} collective-permute-done((f32[256,768]{1,0:T(8,128)S(1)}, f32[256,768]{1,0:T(8,128)S(1)}, u32[]{:S(2)}, u32[]{:S(2)}) %collective-permute-start.4) | collective-permute-done | bytes 786464 | tf_op jit(solution)/shard_map/ppermute | solution.py:24
  281.7 0.1 broadcast_select_fusion.2
  281.8 0.5 stack.3
  282.4 80.0 %all_to_all.5 = f32[8,1,256,768]{3,2,1,0:T(8,128)S(1)} all-to-all(f32[8,1,256,768]{3,2,1,0:T(8,128)S(1)} %stack.3), channel_id=1, replica_groups=mesh['grp'=8,'dom'=32] {'grp'}, dimensions={0} | all-to-all | bytes 12582912 | tf_op jit(solution)/shard_map/all_to_all | solution.py:67
  362.3 2.7 copy.35
  (3 shorter events, 0.0 us)
Async XLA Ops:
  0.0 28.8 %copy-start.1 = (bf16[64,64,64]{2,1,0:T(8,128)(2,1)S(1)}, bf16[64,64,64]{2,1,0:T(8,128)(2,1)}, u32[]{:S(2)}) copy-start(bf16[64,64,64]{2,1,0:T(8,128)(2,1)} %param.6) | copy-start | bytes 1572868
  0.0 40.0 %collective-permute-start = (bf16[64,64,64]{2,1,0:T(8,128)(2,1)}, bf16[64,64,64]{2,1,0:T(8,128)(2,1)S(1)}, u32[]{:S(2)}, u32[]{:S(2)}) collective-permute-start(bf16[64,64,64]{2,1,0:T(8,128)(2,1)} %param.6), channel_id=1, source_target_pairs={{0,1},{1,2},{2,3},{3,4},{4,5},{5,6},{6,7},{7,8},{8,9},{9,10},{10,1... | collective-permute-start | bytes 1572872 | tf_op jit(solution)/shard_map/ppermute | solution.py:14
  2.1 38.9 %collective-permute-start.1 = (bf16[64,64,64]{2,1,0:T(8,128)(2,1)}, bf16[64,64,64]{2,1,0:T(8,128)(2,1)}, u32[]{:S(2)}, u32[]{:S(2)}) collective-permute-start(bf16[64,64,64]{2,1,0:T(8,128)(2,1)} %param.6), channel_id=1, source_target_pairs={{1,0},{2,1},{3,2},{4,3},{5,4},{6,5},{7,6},{8,7},{9,8},{10,9},{11,1... | collective-permute-start | bytes 1572872 | tf_op jit(solution)/shard_map/ppermute | solution.py:17
  40.0 1.0 copy-start.2
  155.8 20.9 %copy-start = (bf16[4096,256]{1,0:T(8,128)(2,1)S(1)}, bf16[4096,256]{1,0:T(8,128)(2,1)}, u32[]{:S(2)}) copy-start(bf16[4096,256]{1,0:T(8,128)(2,1)} %mul.38) | copy-start | bytes 6291460
  181.3 38.4 %collective-permute-start.2 = (f32[256,768]{1,0:T(8,128)S(1)}, f32[256,768]{1,0:T(8,128)S(1)}, u32[]{:S(2)}, u32[]{:S(2)}) collective-permute-start(f32[256,768]{1,0:T(8,128)S(1)} %fusion.25), channel_id=1, source_target_pairs={{0,4},{1,5},{2,6},{3,7},{4,8},{5,9},{6,10},{7,11},{8,12},{9,13},{1... | collective-permute-start | bytes 2359304 | tf_op jit(solution)/shard_map/ppermute | solution.py:24
  219.7 38.2 %collective-permute-start.3 = (f32[256,768]{1,0:T(8,128)S(1)}, f32[256,768]{1,0:T(8,128)S(1)}, u32[]{:S(2)}, u32[]{:S(2)}) collective-permute-start(f32[256,768]{1,0:T(8,128)S(1)} %broadcast_select_fusion), channel_id=1, source_target_pairs={{0,8},{1,9},{2,10},{3,11},{4,12},{5,13},{6,14},{7,15},{8,16},{9,17... | collective-permute-start | bytes 2359304 | tf_op jit(solution)/shard_map/ppermute | solution.py:24
  258.1 23.7 %collective-permute-start.4 = (f32[256,768]{1,0:T(8,128)S(1)}, f32[256,768]{1,0:T(8,128)S(1)}, u32[]{:S(2)}, u32[]{:S(2)}) collective-permute-start(f32[256,768]{1,0:T(8,128)S(1)} %broadcast_select_fusion.1), channel_id=1, source_target_pairs={{0,16},{1,17},{2,18},{3,19},{4,20},{5,21},{6,22},{7,23},{8,24},{9,... | collective-permute-start | bytes 2359304 | tf_op jit(solution)/shard_map/ppermute | solution.py:24
